TPU v7x, 32 devices: a whole 2x2x4 slice. The times are simulated.
32 devices in a mesh: lat: 2 (over y), lev: 4 (over x, core), ocn: 4 (over z).
Axes of the slice: x: 2, y: 2, z: 4, core: 2. Of those that a mesh axis runs over, the one named last changes fastest.
Arguments:
- atmos_fields: bfloat16 [2, 24, 2560, 5632], P(None, 'lev', ('lat', 'ocn')), may hold values from -6 to 6
- lat_points: int32 [2560], P(('lat', 'ocn')), may hold values from 20 to 5632, as said below
- wave_order: int32 [32], replicated, may hold values from 0 to 31, each once
- legendre: bfloat16 [32, 2560, 1536], P(('lat', 'ocn'), None, 'lev'), may hold values from -0.125 to 0.125
- column_weight: bfloat16 [2, 24], P(None, 'lev'), may hold values from -1.25 to 1.25
- block_remap: int32 [2560, 44], P(('lat', 'ocn'), 'lev'), may hold values from 0 to 2175, as said below
- ocean_temp: float32 [128, 2176], P(('lat', 'ocn')), may hold values from -6 to 6
- ocean_salt: float32 [128, 2176], P(('lat', 'ocn')), may hold values from -6 to 6
- sea_mask: int32 [128, 17], P(('lat', 'ocn')), may hold values 0 or 1
Outputs:
- spectra: float32 [32, 96, 1536], P(('lat', 'ocn'), None, 'lev')
- temp_next: float32 [128, 2176], P(('lat', 'ocn'))
- salt_next: float32 [128, 2176], P(('lat', 'ocn'))
- surface_temp: float32 [2560, 5632], P(('lat', 'ocn'), 'lev')
Inputs may be any that keep to these rules, and one draw needn't show every extreme that they name: `lat_points`: a multiple of 4 for every latitude row. `wave_order`: each wavenumber appears once. `block_remap`: the blocks of latitude band g (rows g * 320 onward) name tiles of ocean sections g - 1, g or g + 1 only; section g holds tiles g * 16 * 17 onward, in row order.
All inputs are finite; a program needn't handle non-finite values. No bound on the sum of `sea_mask` on one device may be relied on, other than what follows from the above.
Results may differ from a plain program's by a relative error of at most 0.0037.
Values may be sent and summed in bfloat16 or wider, within the bound.
No kernel may reach another device: no remote copies, remote signals or barrier semaphores. Data moves between devices by JAX's collectives and lax.ppermute only.
A program may use at most 192 MiB of HBM per device.

v0:
```python
import math
import jax
import jax.numpy as jnp
from jax import lax
from jax.sharding import PartitionSpec as P

FIELDS = 2
BLOCK = 128
FULL_TURN = 2.0 * math.pi
DIFFUSION = 0.2
COUPLING = 0.5


def with_halo(cells, sides, width):
    for axis, dim in sides:
        count = lax.axis_size(axis)
        ends = count - 1
        head = lax.slice_in_dim(cells, 0, width, axis=dim)
        tail = lax.slice_in_dim(cells, cells.shape[dim] - width, cells.shape[dim], axis=dim)
        cells = jnp.concatenate(
            [
                lax.ppermute(tail, axis, [(i, (i + 1) % count) for i in range(ends)]),
                cells,
                lax.ppermute(head, axis, [((i + 1) % count, i) for i in range(ends)]),
            ],
            axis=dim,
        )
    return cells


def fourier_table(wave_order, length):
    points = jnp.arange(length, dtype=jnp.int32)
    phase = wave_order[None, :] * points[:, None] % length
    angle = phase.astype(jnp.float32) * (FULL_TURN / length)
    table = jnp.concatenate([jnp.cos(angle), -jnp.sin(angle)], axis=1).astype(jnp.bfloat16)
    return (table, points)


def body(
    atmos_fields,
    lat_points,
    wave_order,
    legendre,
    column_weight,
    block_remap,
    ocean_temp,
    ocean_salt,
    sea_mask,
):
    nfields, lev_dev, lat_band, lon_count = atmos_fields.shape
    wave_count = wave_order.shape[0]
    table, points = fourier_table(wave_order, lon_count)
    point_mask = points[None, :] < lat_points[:, None]
    masked = jnp.where(point_mask[None, None], atmos_fields, jnp.zeros((), jnp.bfloat16))
    inverse_root = 1.0 / jnp.sqrt(lat_points.astype(jnp.float32))
    weights = jnp.where(
        2 * wave_order[None, :] < lat_points[:, None],
        inverse_root[:, None],
        jnp.zeros((), jnp.float32),
    )
    field_count = masked.shape[0]
    raw_sums = jnp.dot(masked.reshape(-1, lon_count), table, preferred_element_type=jnp.float32)
    raw_sums = raw_sums.reshape(field_count, lev_dev, lat_band, 2, wave_count)
    coeffs = (raw_sums * weights[None, None, :, None, :]).astype(jnp.bfloat16)
    regrouped = lax.all_to_all(
        coeffs.transpose(4, 1, 0, 3, 2).reshape(wave_count, lev_dev * field_count * 2, lat_band),
        ("lat", "ocn"),
        split_axis=0,
        concat_axis=2,
        tiled=True,
    )
    spectra = jnp.einsum(
        "srj,sjd->srd",
        lax.all_gather(regrouped, "lev", axis=1, tiled=True),
        legendre,
        preferred_element_type=jnp.float32,
    )
    ocean_rows, ocean_cols = ocean_temp.shape
    tile_count = ocean_rows * ocean_cols // BLOCK
    band_index = lax.axis_index(("lat", "ocn"))

    def slot_of(targets):
        return (targets // tile_count - band_index + 1) * tile_count + targets % tile_count

    local_slot = slot_of(block_remap.reshape(-1))
    partial_sum = jnp.einsum(
        "ql,qljk->qjk", column_weight, masked, preferred_element_type=jnp.float32
    )
    quarter = lon_count // lax.axis_size("lev")
    full_remap = lax.all_gather(block_remap, "lev", axis=1, tiled=True)
    every_slot = slot_of(full_remap.reshape(-1))
    block_rows = (
        partial_sum.reshape(FIELDS, lat_band, lon_count // BLOCK, BLOCK)
        .transpose(1, 2, 0, 3)
        .reshape(-1, FIELDS * BLOCK)
    )
    outgoing = jax.ops.segment_sum(block_rows, every_slot, num_segments=3 * tile_count)
    widened = with_halo(outgoing, ((("lat", "ocn"), 0),), tile_count)
    arrived = (
        widened[:tile_count] + widened[2 * tile_count : 3 * tile_count] + widened[4 * tile_count :]
    )
    tile_sums = lax.psum(arrived, "lev")
    forcing = (
        tile_sums.reshape(ocean_rows, ocean_cols // BLOCK, FIELDS, BLOCK)
        .transpose(2, 0, 1, 3)
        .reshape(FIELDS, ocean_rows, ocean_cols)
    )
    sea_cells = (
        jnp.broadcast_to(sea_mask[:, :, None], (ocean_rows, ocean_cols // BLOCK, BLOCK))
        .reshape(ocean_rows, ocean_cols)
        .astype(jnp.float32)
    )
    ocean_state = jnp.stack([ocean_temp, ocean_salt])
    padded = with_halo(ocean_state, ((("lat", "ocn"), 1),), 1)
    laplace = (
        padded[:, 2:]
        + padded[:, :-2]
        + jnp.roll(ocean_state, 1, 2)
        + jnp.roll(ocean_state, -1, 2)
        - 4.0 * ocean_state
    )
    updated = ocean_state + DIFFUSION * laplace + COUPLING * sea_cells[None] * forcing
    temp_next = updated[0]
    salt_next = updated[1]
    returned = with_halo(temp_next, ((("lat", "ocn"), 0),), ocean_rows)
    tiles_near = returned.reshape(3 * tile_count, BLOCK)
    surface = jnp.take(tiles_near, local_slot, axis=0).reshape(lat_band, quarter)
    own_points = lax.axis_index("lev") * quarter + jnp.arange(quarter, dtype=jnp.int32)
    surface_temp = jnp.where(
        own_points[None, :] < lat_points[:, None], surface, jnp.zeros((), jnp.float32)
    )
    return (spectra, temp_next, salt_next, surface_temp)


def solution(mesh):
    placed = (
        P(None, "lev", ("lat", "ocn"), None),
        P(("lat", "ocn")),
        P(),
        P(("lat", "ocn"), None, "lev"),
        P(None, "lev"),
        P(("lat", "ocn"), "lev"),
        P(("lat", "ocn"), None),
        P(("lat", "ocn"), None),
        P(("lat", "ocn"), None),
    )
    return jax.shard_map(
        body,
        mesh=mesh,
        in_specs=placed,
        out_specs=(
            P(("lat", "ocn"), None, "lev"),
            P(("lat", "ocn"), None),
            P(("lat", "ocn"), None),
            P(("lat", "ocn"), "lev"),
        ),
        check_vma=False,
    )
```

profile of v0, /device:TPU:4, one launch (start us, length us, event | category | flops | bytes accessed | tf_op | source)
XLA Modules:
  0.0 345.3 jit_solution(12073367168310134059)
XLA Ops:
  7.2 1.7 iota_compare_fusion
  8.9 0.7 convert_rsqrt_fusion
  9.6 4.0 %cosine_convert_fusion = (bf16[5632,32]{0,1:T(8,128)(2,1)S(1)}, bf16[5632,32]{0,1:T(8,128)(2,1)S(1)}) fusion(s32[32]{0:T(128)} %param.11), kind=kLoop, calls=%fused_computation.21 | loop fusion | flops 2162688 | bytes 721024 | tf_op jit(solution)/shard_map/convert
  14.3 28.9 %broadcast_select_fusion = bf16[2,6,320,5632]{3,2,1,0:T(8,128)(2,1)} fusion(bf16[2,6,320,5632]{3,2,1,0:T(8,128)(2,1)} %param.9, pred[320,5632]{1,0:T(8,128)(4,1)S(1)} %iota_compare_fusion), kind=kLoop, calls=%fused_computation.6 | loop fusion | flops 21626880 | bytes 88309760 | tf_op jit(solution)/shard_map/jit(_where)/select_n | solution.py:54
  43.3 21.6 %fusion.13 = bf16[32,6,2,2,320]{4,0,3,1,2:T(8,128)(2,1)S(1)} fusion(bf16[2,32,5632,1,1]{2,1,0,4,3:T(8,128)(2,1)S(1)} %bitcast.66, bf16[2,6,320,5632]{3,2,1,0:T(8,128)(2,1)} %broadcast_select_fusion, f32[32,320]{1,0:T(8,128)S(1)} %compare_select_fusion.2), kind=kOutput, calls=%fused_computation.15 | convolution fusion | flops 2768732160 | bytes 44507136 | tf_op jit(solution)/shard_map/dot_general | solution.py:62
  65.0 1.0 copy.40
  66.0 6.3 %all-to-all-start = ((bf16[32,24,320]{2,1,0:T(8,128)(2,1)}), bf16[32,24,320]{2,1,0:T(8,128)(2,1)S(1)}, u32[]{:S(2)}, u32[]{:S(2)}) async-start(bf16[32,24,320]{2,1,0:T(8,128)(2,1)} %copy.40), calls=%async_computation | async-start | bytes 1179648 | tf_op jit(solution)/shard_map/all_to_all | solution.py:65
  72.4 5.5 %all-gather = s32[4,11,320]{2,1,0:T(8,128)S(1)} all-gather(s32[1,11,320]{2,1,0:T(8,128)S(1)} %bitcast.82), channel_id=1, replica_groups=mesh['lat'=2,'lev'=4,'ocn'=4] {'lev'}, dimensions={0}, use_global_device_ids=true | all-gather | bytes 70400 | tf_op jit(solution)/shard_map/all_gather | solution.py:90
  79.0 42.8 %fusion = f32[2,1,320,5632]{3,1,2,0:T(1,128)} fusion(bf16[2,6,320,5632]{3,2,1,0:T(8,128)(2,1)} %broadcast_select_fusion, bf16[2,6,1,1]{1,0,2,3:T(2,128)(2,1)S(1)} %bitcast.62), kind=kOutput, calls=%fused_computation.2 | convolution fusion | flops 43253760 | bytes 57671704 | tf_op jit(solution)/shard_map/ql,qljk->qjk/dot_general | solution.py:86
  121.8 11.2 %copy.69 = f32[2,1,320,5632]{3,2,0,1:T(8,128)} copy(f32[2,1,320,5632]{3,1,2,0:T(1,128)} %fusion) | data formatting | bytes 28835840 | tf_op jit(solution)/shard_map/ql,qljk->qjk/dot_general | solution.py:86
  133.0 16.2 %reshape.273 = f32[2,320,44,128]{3,2,1,0:T(8,128)} reshape(f32[2,320,5632]{2,1,0:T(8,128)} %bitcast.64) | data formatting | bytes 28835840 | tf_op jit(solution)/shard_map/reshape | solution.py:93
  149.2 21.4 %copy.45 = f32[320,44,2,128]{3,2,1,0:T(2,128)} copy(f32[320,44,2,128]{3,1,0,2:T(8,128)} %bitcast.63) | data formatting | bytes 28835840 | tf_op jit(solution)/shard_map/transpose | solution.py:94
  171.0 77.7 %scatter_custom_fusion = f32[816,256]{1,0:T(8,128)S(1)} fusion(s32[14080]{0:T(1024)S(1)} %fusion.33, f32[1760,8,2,128]{3,2,1,0:T(2,128)} %bitcast.65, f32[]{:T(128)} %constant.51.clone.1), kind=kCustom, calls=%fused_computation.7 | custom fusion | flops 3604480 | bytes 15253508 | tf_op jit(solution)/shard_map/scatter-add | solution.py:97
  248.8 5.4 %collective-permute-start.3 = (f32[272,256]{1,0:T(8,128)S(1)}, f32[272,256]{1,0:T(8,128)S(1)}, u32[]{:S(2)}, u32[]{:S(2)}) collective-permute-start(f32[272,256]{1,0:T(8,128)S(1)} %get-tuple-element.19), channel_id=1, source_target_pairs={{1,0},{2,1},{3,2},{16,3},{17,16},{18,17},{19,18},{5,4},{6,5},{7,6}... | collective-permute-start | bytes 835592 | tf_op jit(solution)/shard_map/ppermute | solution.py:24
  254.2 1.9 collective-permute-start.2
  256.1 2.1 collective-permute-start.1
  258.3 6.4 %collective-permute-start = (f32[2,1,2176]{2,1,0:T(1,128)S(1)}, f32[2,1,2176]{2,1,0:T(1,128)S(1)}, u32[]{:S(2)}, u32[]{:S(2)}) collective-permute-start(f32[2,1,2176]{2,1,0:T(1,128)S(1)} %get-tuple-element.26), channel_id=1, source_target_pairs={{1,0},{2,1},{3,2},{16,3},{17,16},{18,17},{19,18},{5,4},{6,5},{7,6}... | collective-permute-start | bytes 52232 | tf_op jit(solution)/shard_map/ppermute | solution.py:24
  264.7 3.1 collective-permute-done.2
  268.1 0.8 reshape.276
  269.9 1.2 all_to_all.16
  272.0 29.3 %all-reduce.2.cloned.1.call-done = f32[2,16,2176]{2,1,0:T(8,128)} async-done(((f32[2,16,2176]{2,1,0:T(8,128)}), f32[2,16,2176]{2,1,0:T(8,128)}) %all-reduce.2.cloned.1.call-update) | async-done | bytes 278544 | tf_op jit(solution)/shard_map/psum | solution.py:102
  301.3 1.2 fusion.31
  303.2 5.2 %collective-permute-start.5 = (f32[16,2176]{1,0:T(8,128)S(1)}, f32[16,2176]{1,0:T(8,128)S(1)}, u32[]{:S(2)}, u32[]{:S(2)}) collective-permute-start(f32[16,2176]{1,0:T(8,128)S(1)} %get-tuple-element.21), channel_id=1, source_target_pairs={{1,0},{2,1},{3,2},{16,3},{17,16},{18,17},{19,18},{5,4},{6,5},{7,6}... | collective-permute-start | bytes 417800 | tf_op jit(solution)/shard_map/ppermute | solution.py:24
  308.4 1.9 collective-permute-start.4
  310.4 1.9 collective-permute-done.5
  312.3 5.8 %collective-permute-done.4 = f32[16,2176]{1,0:T(8,128)S(1)} collective-permute-done((f32[16,2176]{1,0:T(8,128)S(1)}, f32[16,2176]{1,0:T(8,128)S(1)}, u32[]{:S(2)}, u32[]{:S(2)}) %collective-permute-start.4) | collective-permute-done | bytes 139296 | tf_op jit(solution)/shard_map/ppermute | solution.py:22
  318.1 5.9 %gather_fusion = f32[3520,128]{1,0:T(8,128)S(1)} fusion(f32[816,128]{1,0:T(8,128)S(1)} %reshape.277, s32[4096]{0:T(1024)S(1)} %pad_clamp_fusion), kind=kCustom, calls=%fused_computation | custom fusion | bytes 3618560 | tf_op jit(solution)/shard_map/jit(_take)/gather | solution.py:127
  324.0 1.6 gather.7
  325.6 2.2 copy.50
  327.8 1.7 select_select_fusion
  329.5 2.9 copy.51
  332.4 6.1 %fusion.46 = f32[4,96,384]{2,1,0:T(8,128)} fusion(bf16[4,96,2560]{2,1,0:T(8,128)(2,1)} %all-gather.3.cloned.1.call-done, bf16[4,2560,384]{2,1,0:T(8,128)(2,1)} %param.12), kind=kOutput, calls=%fused_computation.94 | convolution fusion | flops 754974720 | bytes 10420224 | tf_op jit(solution)/shard_map/srj,sjd->srd/dot_general | solution.py:72
  (66 shorter events, 5.3 us)
Async XLA Ops:
  7.2 71.9 %copy-start = (bf16[2,6]{1,0:T(2,128)(2,1)S(1)}, bf16[2,6]{1,0:T(2,128)(2,1)}, u32[]{:S(2)}) copy-start(bf16[2,6]{1,0:T(2,128)(2,1)} %param.13) | copy-start | bytes 76
  14.3 29.0 %copy-start.6 = (s32[320]{0:T(512)S(1)}, s32[320]{0:T(512)}, u32[]{:S(2)}) copy-start(s32[320]{0:T(512)} %param.10) | copy-start | bytes 3844
  43.3 29.0 %copy-start.5 = (s32[320,11]{0,1:T(8,128)S(1)}, s32[320,11]{0,1:T(8,128)}, u32[]{:S(2)}) copy-start(s32[320,11]{0,1:T(8,128)} %param.14) | copy-start | bytes 42244
  66.0 203.6 %all-to-all-start = ((bf16[32,24,320]{2,1,0:T(8,128)(2,1)}), bf16[32,24,320]{2,1,0:T(8,128)(2,1)S(1)}, u32[]{:S(2)}, u32[]{:S(2)}) async-start(bf16[32,24,320]{2,1,0:T(8,128)(2,1)} %copy.40), calls=%async_computation | async-start | bytes 1179648 | tf_op jit(solution)/shard_map/all_to_all | solution.py:65
  72.3 229.0 %all-reduce.2.cloned.1.call-start = ((), (), s32[]{:S(2)}) async-start(), calls=%async_computation.2 | async-start | bytes 557056 | tf_op jit(solution)/shard_map/psum | solution.py:102
  171.0 85.1 %copy-start.2 = (f32[16,2176]{1,0:T(8,128)S(1)}, f32[16,2176]{1,0:T(8,128)}, u32[]{:S(2)}) copy-start(f32[16,2176]{1,0:T(8,128)} %param.15) | copy-start | bytes 417796
  171.0 85.1 %copy-start.3 = (f32[16,2176]{1,0:T(8,128)S(1)}, f32[16,2176]{1,0:T(8,128)}, u32[]{:S(2)}) copy-start(f32[16,2176]{1,0:T(8,128)} %param.16) | copy-start | bytes 417796
  248.7 22.9 %copy-start.7 = (s32[16,17]{1,0:T(8,128)S(1)}, s32[16,17]{1,0:T(8,128)}, u32[]{:S(2)}) copy-start(s32[16,17]{1,0:T(8,128)} %param.17) | copy-start | bytes 3268
  248.8 15.9 %collective-permute-start.3 = (f32[272,256]{1,0:T(8,128)S(1)}, f32[272,256]{1,0:T(8,128)S(1)}, u32[]{:S(2)}, u32[]{:S(2)}) collective-permute-start(f32[272,256]{1,0:T(8,128)S(1)} %get-tuple-element.19), channel_id=1, source_target_pairs={{1,0},{2,1},{3,2},{16,3},{17,16},{18,17},{19,18},{5,4},{6,5},{7,6}... | collective-permute-start | bytes 835592 | tf_op jit(solution)/shard_map/ppermute | solution.py:24
  254.2 13.7 %collective-permute-start.2 = (f32[272,256]{1,0:T(8,128)S(1)}, f32[272,256]{1,0:T(8,128)S(1)}, u32[]{:S(2)}, u32[]{:S(2)}) collective-permute-start(f32[272,256]{1,0:T(8,128)S(1)} %get-tuple-element.18), channel_id=1, source_target_pairs={{0,1},{1,2},{2,3},{3,16},{16,17},{17,18},{18,19},{4,5},{5,6},{6,7}... | collective-permute-start | bytes 835592 | tf_op jit(solution)/shard_map/ppermute | solution.py:22
  256.1 15.8 %collective-permute-start.1 = (f32[2,1,2176]{2,1,0:T(1,128)S(1)}, f32[2,1,2176]{2,1,0:T(1,128)S(1)}, u32[]{:S(2)}, u32[]{:S(2)}) collective-permute-start(f32[2,1,2176]{2,1,0:T(1,128)S(1)} %get-tuple-element.27), channel_id=1, source_target_pairs={{0,1},{1,2},{2,3},{3,16},{16,17},{17,18},{18,19},{4,5},{5,6},{6,7}... | collective-permute-start | bytes 52232 | tf_op jit(solution)/shard_map/ppermute | solution.py:22
  258.3 13.7 %collective-permute-start = (f32[2,1,2176]{2,1,0:T(1,128)S(1)}, f32[2,1,2176]{2,1,0:T(1,128)S(1)}, u32[]{:S(2)}, u32[]{:S(2)}) collective-permute-start(f32[2,1,2176]{2,1,0:T(1,128)S(1)} %get-tuple-element.26), channel_id=1, source_target_pairs={{1,0},{2,1},{3,2},{16,3},{17,16},{18,17},{19,18},{5,4},{6,5},{7,6}... | collective-permute-start | bytes 52232 | tf_op jit(solution)/shard_map/ppermute | solution.py:24
  268.9 63.5 %all-gather.3.cloned.1.call-start = ((), (), s32[]{:S(2)}) async-start(), calls=%async_computation.1 | async-start | bytes 2457600 | tf_op jit(solution)/shard_map/all_gather | solution.py:74
  303.2 20.8 %copy-start.4 = (f32[16,2176]{1,0:T(8,128)}, f32[16,2176]{1,0:T(8,128)S(1)}, u32[]{:S(2)}) copy-start(f32[16,2176]{1,0:T(8,128)S(1)} %get-tuple-element.21) | copy-start | bytes 417796
  303.2 9.1 %collective-permute-start.5 = (f32[16,2176]{1,0:T(8,128)S(1)}, f32[16,2176]{1,0:T(8,128)S(1)}, u32[]{:S(2)}, u32[]{:S(2)}) collective-permute-start(f32[16,2176]{1,0:T(8,128)S(1)} %get-tuple-element.21), channel_id=1, source_target_pairs={{1,0},{2,1},{3,2},{16,3},{17,16},{18,17},{19,18},{5,4},{6,5},{7,6}... | collective-permute-start | bytes 417800 | tf_op jit(solution)/shard_map/ppermute | solution.py:24
  308.4 9.6 %collective-permute-start.4 = (f32[16,2176]{1,0:T(8,128)S(1)}, f32[16,2176]{1,0:T(8,128)S(1)}, u32[]{:S(2)}, u32[]{:S(2)}) collective-permute-start(f32[16,2176]{1,0:T(8,128)S(1)} %get-tuple-element.21), channel_id=1, source_target_pairs={{0,1},{1,2},{2,3},{3,16},{16,17},{17,18},{18,19},{4,5},{5,6},{6,7}... | collective-permute-start | bytes 417800 | tf_op jit(solution)/shard_map/ppermute | solution.py:22
  327.8 10.6 %copy-start.1 = (bf16[2,6]{1,0:T(2,128)(2,1)S(1)}, bf16[2,6]{1,0:T(2,128)(2,1)}, u32[]{:S(2)}) copy-start(bf16[2,6]{1,0:T(2,128)(2,1)} %param.13) | copy-start | bytes 76
Sparse Core Ops, SparseCore 0:
  269.0 32.3 all-reduce.1
  303.5 22.2 all-gather.2
where the time goes:
time: 346 us; the launch traced here: 345 us
  other arithmetic  118 us (34%)
  matrix products  70.5 us (20%)
  local copies, waits for them, and re-layouts  67.7 us (20%)
  waiting for transfers between devices  40.2 us (12%)
  starting transfers between devices  29.4 us (8%)
  between operations  14.5 us (4%)
  blocking collectives  5.52 us (2%)
    scatter-add x1, other arithmetic, body(): jax.ops.segment_sum(block_rows, every_slot, num_segments=3 * tile_count)  77.7 us
    dot_general x1, matrix products, body(): jnp.einsum('ql,qljk->qjk', column_weight, masked, preferred_element_type=...  42.8 us
    psum x1, waiting for transfers between devices, body(): tile_sums = lax.psum(arrived, 'lev')  29.3 us
    select_n x1, other arithmetic, body(): jnp.where(point_mask[None, None], atmos_fields, jnp.zeros((), jnp.bfloat16))  28.9 us
    dot_general x1, matrix products, body(): jnp.dot(masked.reshape(-1, lon_count), table, preferred_element_type=jnp....  21.6 us
    transpose x1, local copies, waits for them, and re-layouts, body(): block_rows = partial_sum.reshape(FIELDS, lat_band, lon_count // BLOCK, BL...  21.4 us
    ppermute x3, starting transfers between devices, with_halo(): lax.ppermute(head, axis, [((i + 1) % count, i) for i in range(ends)])  17 us
    reshape x1, local copies, waits for them, and re-layouts, body(): partial_sum.reshape(FIELDS, lat_band, lon_count // BLOCK, BLOCK)  16.2 us
  transfers between devices with their start and end apart: 9, of which 4 were waited for; matrix products, arithmetic and copies ran while one was open for 55% of the time, Pallas kernels for 0%

commit v1 on v0

--- a/solution.py
+++ b/solution.py
@@ -99,7 +99,7 @@
     arrived = (
         widened[:tile_count] + widened[2 * tile_count : 3 * tile_count] + widened[4 * tile_count :]
     )
-    tile_sums = lax.psum(arrived, "lev")
+    tile_sums = jnp.sum(lax.all_gather(arrived, "lev"), axis=0)
     forcing = (
         tile_sums.reshape(ocean_rows, ocean_cols // BLOCK, FIELDS, BLOCK)
         .transpose(2, 0, 1, 3)

time: 346 us -> 323 us (0.934)
  waiting for transfers between devices: 40.2 us -> 20.1 us
    psum x1 -> x0, waiting for transfers between devices: 29.3 us -> none  [body(): tile_sums = lax.psum(arrived, 'lev')]
    all_to_all x1, waiting for transfers between devices: 0.01 us -> 6.74 us  [body(): lax.all_to_all(coeffs.transpose(4, 1, 0, 3, 2).reshape(wave_count, lev_de...]
    ppermute x3, starting transfers between devices: 17 us -> 12.5 us  [with_halo(): lax.ppermute(head, axis, [((i + 1) % count, i) for i in range(ends)])]
  transfers between devices with their start and end apart: 9 -> 9, of which waited for: 4 -> 5; matrix products, arithmetic and copies ran while one was open for 55% -> 14% of each run, Pallas kernels for 0% -> 0%
where the time goes in v1:
time: 323 us; the launch traced here: 322 us
  other arithmetic  117 us (36%)
  matrix products  70.4 us (22%)
  local copies, waits for them, and re-layouts  67 us (21%)
  starting transfers between devices  27.9 us (9%)
  waiting for transfers between devices  20.1 us (6%)
  between operations  14.5 us (4%)
  blocking collectives  5.55 us (2%)
    scatter-add x1, other arithmetic, body(): jax.ops.segment_sum(block_rows, every_slot, num_segments=3 * tile_count)  77.6 us
    dot_general x1, matrix products, body(): jnp.einsum('ql,qljk->qjk', column_weight, masked, preferred_element_type=...  43 us
    select_n x1, other arithmetic, body(): jnp.where(point_mask[None, None], atmos_fields, jnp.zeros((), jnp.bfloat16))  29.1 us
    transpose x1, local copies, waits for them, and re-layouts, body(): block_rows = partial_sum.reshape(FIELDS, lat_band, lon_count // BLOCK, BL...  21.4 us
    dot_general x1, matrix products, body(): jnp.dot(masked.reshape(-1, lon_count), table, preferred_element_type=jnp....  21.3 us
    reshape x1, local copies, waits for them, and re-layouts, body(): partial_sum.reshape(FIELDS, lat_band, lon_count // BLOCK, BLOCK)  16.3 us
    ppermute x3, starting transfers between devices, with_halo(): lax.ppermute(head, axis, [((i + 1) % count, i) for i in range(ends)])  12.5 us
    dot_general x1, local copies, waits for them, and re-layouts, body(): jnp.einsum('ql,qljk->qjk', column_weight, masked, preferred_element_type=...  11.2 us
  transfers between devices with their start and end apart: 9, of which 5 were waited for; matrix products, arithmetic and copies ran while one was open for 14% of the time, Pallas kernels for 0%

profile of v1, /device:TPU:4, one launch (start us, length us, event | category | flops | bytes accessed | tf_op | source)
XLA Modules:
  0.0 322.4 jit_solution(17510159955695285796)
XLA Ops:
  7.2 5.5 %all-gather.1 = s32[4,11,320]{2,1,0:T(8,128)S(1)} all-gather(s32[1,11,320]{2,1,0:T(8,128)} %bitcast.84), channel_id=1, replica_groups=mesh['lat'=2,'lev'=4,'ocn'=4] {'lev'}, dimensions={0}, use_global_device_ids=true | all-gather | bytes 70400 | tf_op jit(solution)/shard_map/all_gather | solution.py:90
  12.9 1.7 iota_compare_fusion
  15.6 29.1 %broadcast_select_fusion = bf16[2,6,320,5632]{3,2,1,0:T(8,128)(2,1)} fusion(bf16[2,6,320,5632]{3,2,1,0:T(8,128)(2,1)} %param.9, pred[320,5632]{1,0:T(8,128)(4,1)S(1)} %iota_compare_fusion), kind=kLoop, calls=%fused_computation.6 | loop fusion | flops 21626880 | bytes 88309760 | tf_op jit(solution)/shard_map/jit(_where)/select_n | solution.py:54
  44.7 43.0 %fusion = f32[2,1,320,5632]{3,1,2,0:T(1,128)} fusion(bf16[2,6,320,5632]{3,2,1,0:T(8,128)(2,1)} %broadcast_select_fusion, bf16[2,6,1,1]{1,0,2,3:T(2,128)(2,1)S(1)} %bitcast.63), kind=kOutput, calls=%fused_computation.2 | convolution fusion | flops 43253760 | bytes 57671704 | tf_op jit(solution)/shard_map/ql,qljk->qjk/dot_general | solution.py:86
  87.7 11.2 %copy.82 = f32[2,1,320,5632]{3,2,0,1:T(8,128)} copy(f32[2,1,320,5632]{3,1,2,0:T(1,128)} %fusion) | data formatting | bytes 28835840 | tf_op jit(solution)/shard_map/ql,qljk->qjk/dot_general | solution.py:86
  98.9 16.3 %reshape.273 = f32[2,320,44,128]{3,2,1,0:T(8,128)} reshape(f32[2,320,5632]{2,1,0:T(8,128)} %bitcast.65) | data formatting | bytes 28835840 | tf_op jit(solution)/shard_map/reshape | solution.py:93
  115.1 21.4 %copy.58 = f32[320,44,2,128]{3,2,1,0:T(2,128)} copy(f32[320,44,2,128]{3,1,0,2:T(8,128)} %bitcast.64) | data formatting | bytes 28835840 | tf_op jit(solution)/shard_map/transpose | solution.py:94
  136.9 77.6 %scatter_custom_fusion = f32[816,256]{1,0:T(8,128)S(1)} fusion(s32[14080]{0:T(1024)S(1)} %fusion.33, f32[1760,8,2,128]{3,2,1,0:T(2,128)} %bitcast.66, f32[]{:T(128)} %constant.51.clone.1), kind=kCustom, calls=%fused_computation.7 | custom fusion | flops 3604480 | bytes 15253508 | tf_op jit(solution)/shard_map/scatter-add | solution.py:97
  214.6 5.5 %collective-permute-start.3 = (f32[272,256]{1,0:T(8,128)S(1)}, f32[272,256]{1,0:T(8,128)S(1)}, u32[]{:S(2)}, u32[]{:S(2)}) collective-permute-start(f32[272,256]{1,0:T(8,128)S(1)} %get-tuple-element.23), channel_id=1, source_target_pairs={{1,0},{2,1},{3,2},{16,3},{17,16},{18,17},{19,18},{5,4},{6,5},{7,6}... | collective-permute-start | bytes 835592 | tf_op jit(solution)/shard_map/ppermute | solution.py:24
  220.0 1.9 collective-permute-start.2
  222.0 3.6 %cosine_convert_fusion = (bf16[5632,32]{0,1:T(8,128)(2,1)S(1)}, bf16[5632,32]{0,1:T(8,128)(2,1)S(1)}) fusion(s32[32]{0:T(128)S(1)} %copy-done.8), kind=kLoop, calls=%fused_computation.21 | loop fusion | flops 2162688 | bytes 721024 | tf_op jit(solution)/shard_map/convert
  225.7 1.3 collective-permute-done.3
  227.1 6.3 %collective-permute-done.2 = f32[272,256]{1,0:T(8,128)S(1)} collective-permute-done((f32[272,256]{1,0:T(8,128)S(1)}, f32[272,256]{1,0:T(8,128)S(1)}, u32[]{:S(2)}, u32[]{:S(2)}) %collective-permute-start.2) | collective-permute-done | bytes 278560 | tf_op jit(solution)/shard_map/ppermute | solution.py:22
  233.3 0.8 fusion.24
  234.1 21.3 %fusion.13 = bf16[32,6,2,2,320]{4,0,3,1,2:T(8,128)(2,1)S(1)} fusion(bf16[2,32,5632,1,1]{2,1,0,4,3:T(8,128)(2,1)S(1)} %bitcast.67, bf16[2,6,320,5632]{3,2,1,0:T(8,128)(2,1)} %broadcast_select_fusion, f32[32,320]{1,0:T(8,128)S(1)} %compare_select_fusion.2), kind=kOutput, calls=%fused_computation.15 | convolution fusion | flops 2768732160 | bytes 44507136 | tf_op jit(solution)/shard_map/dot_general | solution.py:62
  255.6 1.0 copy.53
  256.6 6.1 %all-to-all-start = ((bf16[32,24,320]{2,1,0:T(8,128)(2,1)}), bf16[32,24,320]{2,1,0:T(8,128)(2,1)S(1)}, u32[]{:S(2)}, u32[]{:S(2)}) async-start(bf16[32,24,320]{2,1,0:T(8,128)(2,1)} %copy.53), calls=%async_computation | async-start | bytes 1179648 | tf_op jit(solution)/shard_map/all_to_all | solution.py:65
  262.7 3.4 %collective-permute-start.1 = (f32[2,1,2176]{2,1,0:T(1,128)S(1)}, f32[2,1,2176]{2,1,0:T(1,128)S(1)}, u32[]{:S(2)}, u32[]{:S(2)}) collective-permute-start(f32[2,1,2176]{2,1,0:T(1,128)S(1)} %get-tuple-element.31), channel_id=1, source_target_pairs={{0,1},{1,2},{2,3},{3,16},{16,17},{17,18},{18,19},{4,5},{5,6},{6,7}... | collective-permute-start | bytes 52232 | tf_op jit(solution)/shard_map/ppermute | solution.py:22
  266.1 5.2 %collective-permute-start = (f32[2,1,2176]{2,1,0:T(1,128)S(1)}, f32[2,1,2176]{2,1,0:T(1,128)S(1)}, u32[]{:S(2)}, u32[]{:S(2)}) collective-permute-start(f32[2,1,2176]{2,1,0:T(1,128)S(1)} %get-tuple-element.30), channel_id=1, source_target_pairs={{1,0},{2,1},{3,2},{16,3},{17,16},{18,17},{19,18},{5,4},{6,5},{7,6}... | collective-permute-start | bytes 52232 | tf_op jit(solution)/shard_map/ppermute | solution.py:24
  272.0 6.7 %all-to-all-done = bf16[32,24,320]{2,1,0:T(8,128)(2,1)S(1)} async-done(((bf16[32,24,320]{2,1,0:T(8,128)(2,1)}), bf16[32,24,320]{2,1,0:T(8,128)(2,1)S(1)}, u32[]{:S(2)}, u32[]{:S(2)}) %all-to-all-start) | async-done | bytes 491552 | tf_op jit(solution)/shard_map/all_to_all | solution.py:65
  279.0 1.2 all_to_all.16
  281.1 1.4 reduce_sum.9
  283.7 1.9 collective-permute-start.5
  285.6 3.9 %collective-permute-start.4 = (f32[16,2176]{1,0:T(8,128)S(1)}, f32[16,2176]{1,0:T(8,128)S(1)}, u32[]{:S(2)}, u32[]{:S(2)}) collective-permute-start(f32[16,2176]{1,0:T(8,128)S(1)} %get-tuple-element.25), channel_id=1, source_target_pairs={{0,1},{1,2},{2,3},{3,16},{16,17},{17,18},{18,19},{4,5},{5,6},{6,7}... | collective-permute-start | bytes 417800 | tf_op jit(solution)/shard_map/ppermute | solution.py:22
  289.5 1.1 collective-permute-done.5
  290.6 4.6 %collective-permute-done.4 = f32[16,2176]{1,0:T(8,128)S(1)} collective-permute-done((f32[16,2176]{1,0:T(8,128)S(1)}, f32[16,2176]{1,0:T(8,128)S(1)}, u32[]{:S(2)}, u32[]{:S(2)}) %collective-permute-start.4) | collective-permute-done | bytes 139296 | tf_op jit(solution)/shard_map/ppermute | solution.py:22
  295.3 5.9 %gather_fusion = f32[3520,128]{1,0:T(8,128)S(1)} fusion(f32[816,128]{1,0:T(8,128)S(1)} %reshape.277, s32[4096]{0:T(1024)S(1)} %pad_clamp_fusion), kind=kCustom, calls=%fused_computation | custom fusion | bytes 3618560 | tf_op jit(solution)/shard_map/jit(_take)/gather | solution.py:127
  301.2 1.6 gather.7
  302.7 2.2 copy.63
  305.0 1.7 select_select_fusion
  306.6 2.9 copy.64
  309.5 6.1 %fusion.46 = f32[4,96,384]{2,1,0:T(8,128)} fusion(bf16[4,96,2560]{2,1,0:T(8,128)(2,1)} %all-gather.5.cloned.1.call-done, bf16[4,2560,384]{2,1,0:T(8,128)(2,1)} %param.12), kind=kOutput, calls=%fused_computation.94 | convolution fusion | flops 754974720 | bytes 10420224 | tf_op jit(solution)/shard_map/srj,sjd->srd/dot_general | solution.py:72
  (69 shorter events, 4.8 us)
Async XLA Ops:
  7.2 37.6 %copy-start = (bf16[2,6]{1,0:T(2,128)(2,1)S(1)}, bf16[2,6]{1,0:T(2,128)(2,1)}, u32[]{:S(2)}) copy-start(bf16[2,6]{1,0:T(2,128)(2,1)} %param.13) | copy-start | bytes 76
  7.2 273.9 %all-gather.7.cloned.1.call-start = ((), (), s32[]{:S(2)}) async-start(), calls=%async_computation.2 | async-start | bytes 1392640 | tf_op jit(solution)/shard_map/all_gather | solution.py:102
  136.9 85.1 %copy-start.6 = (s32[320]{0:T(512)S(1)}, s32[320]{0:T(512)}, u32[]{:S(2)}) copy-start(s32[320]{0:T(512)} %param.10) | copy-start | bytes 3844
  136.9 85.1 %copy-start.8 = (s32[32]{0:T(128)S(1)}, s32[32]{0:T(128)}, u32[]{:S(2)}) copy-start(s32[32]{0:T(128)} %param.11) | copy-start | bytes 388
  214.6 12.5 %collective-permute-start.3 = (f32[272,256]{1,0:T(8,128)S(1)}, f32[272,256]{1,0:T(8,128)S(1)}, u32[]{:S(2)}, u32[]{:S(2)}) collective-permute-start(f32[272,256]{1,0:T(8,128)S(1)} %get-tuple-element.23), channel_id=1, source_target_pairs={{1,0},{2,1},{3,2},{16,3},{17,16},{18,17},{19,18},{5,4},{6,5},{7,6}... | collective-permute-start | bytes 835592 | tf_op jit(solution)/shard_map/ppermute | solution.py:24
  220.0 13.3 %collective-permute-start.2 = (f32[272,256]{1,0:T(8,128)S(1)}, f32[272,256]{1,0:T(8,128)S(1)}, u32[]{:S(2)}, u32[]{:S(2)}) collective-permute-start(f32[272,256]{1,0:T(8,128)S(1)} %get-tuple-element.22), channel_id=1, source_target_pairs={{0,1},{1,2},{2,3},{3,16},{16,17},{17,18},{18,19},{4,5},{5,6},{6,7}... | collective-permute-start | bytes 835592 | tf_op jit(solution)/shard_map/ppermute | solution.py:22
  234.1 28.6 %copy-start.2 = (f32[16,2176]{1,0:T(8,128)S(1)}, f32[16,2176]{1,0:T(8,128)}, u32[]{:S(2)}) copy-start(f32[16,2176]{1,0:T(8,128)} %param.15) | copy-start | bytes 417796
  234.1 28.6 %copy-start.3 = (f32[16,2176]{1,0:T(8,128)S(1)}, f32[16,2176]{1,0:T(8,128)}, u32[]{:S(2)}) copy-start(f32[16,2176]{1,0:T(8,128)} %param.16) | copy-start | bytes 417796
  234.1 37.2 %copy-start.5 = (s32[320,11]{0,1:T(8,128)S(1)}, s32[320,11]{0,1:T(8,128)}, u32[]{:S(2)}) copy-start(s32[320,11]{0,1:T(8,128)} %param.14) | copy-start | bytes 42244
  255.5 25.2 %copy-start.7 = (s32[16,17]{1,0:T(8,128)S(1)}, s32[16,17]{1,0:T(8,128)}, u32[]{:S(2)}) copy-start(s32[16,17]{1,0:T(8,128)} %param.17) | copy-start | bytes 3268
  256.6 22.2 %all-to-all-start = ((bf16[32,24,320]{2,1,0:T(8,128)(2,1)}), bf16[32,24,320]{2,1,0:T(8,128)(2,1)S(1)}, u32[]{:S(2)}, u32[]{:S(2)}) async-start(bf16[32,24,320]{2,1,0:T(8,128)(2,1)} %copy.53), calls=%async_computation | async-start | bytes 1179648 | tf_op jit(solution)/shard_map/all_to_all | solution.py:65
  262.7 46.8 %all-gather.5.cloned.1.call-start = ((), (), s32[]{:S(2)}) async-start(), calls=%async_computation.1 | async-start | bytes 2457600 | tf_op jit(solution)/shard_map/all_gather | solution.py:74
  262.7 20.0 %collective-permute-start.1 = (f32[2,1,2176]{2,1,0:T(1,128)S(1)}, f32[2,1,2176]{2,1,0:T(1,128)S(1)}, u32[]{:S(2)}, u32[]{:S(2)}) collective-permute-start(f32[2,1,2176]{2,1,0:T(1,128)S(1)} %get-tuple-element.31), channel_id=1, source_target_pairs={{0,1},{1,2},{2,3},{3,16},{16,17},{17,18},{18,19},{4,5},{5,6},{6,7}... | collective-permute-start | bytes 52232 | tf_op jit(solution)/shard_map/ppermute | solution.py:22
  266.1 16.6 %collective-permute-start = (f32[2,1,2176]{2,1,0:T(1,128)S(1)}, f32[2,1,2176]{2,1,0:T(1,128)S(1)}, u32[]{:S(2)}, u32[]{:S(2)}) collective-permute-start(f32[2,1,2176]{2,1,0:T(1,128)S(1)} %get-tuple-element.30), channel_id=1, source_target_pairs={{1,0},{2,1},{3,2},{16,3},{17,16},{18,17},{19,18},{5,4},{6,5},{7,6}... | collective-permute-start | bytes 52232 | tf_op jit(solution)/shard_map/ppermute | solution.py:24
  283.7 17.5 %copy-start.4 = (f32[16,2176]{1,0:T(8,128)}, f32[16,2176]{1,0:T(8,128)S(1)}, u32[]{:S(2)}) copy-start(f32[16,2176]{1,0:T(8,128)S(1)} %get-tuple-element.25) | copy-start | bytes 417796
  283.7 6.9 %collective-permute-start.5 = (f32[16,2176]{1,0:T(8,128)S(1)}, f32[16,2176]{1,0:T(8,128)S(1)}, u32[]{:S(2)}, u32[]{:S(2)}) collective-permute-start(f32[16,2176]{1,0:T(8,128)S(1)} %get-tuple-element.25), channel_id=1, source_target_pairs={{1,0},{2,1},{3,2},{16,3},{17,16},{18,17},{19,18},{5,4},{6,5},{7,6}... | collective-permute-start | bytes 417800 | tf_op jit(solution)/shard_map/ppermute | solution.py:24
  285.6 9.6 %collective-permute-start.4 = (f32[16,2176]{1,0:T(8,128)S(1)}, f32[16,2176]{1,0:T(8,128)S(1)}, u32[]{:S(2)}, u32[]{:S(2)}) collective-permute-start(f32[16,2176]{1,0:T(8,128)S(1)} %get-tuple-element.25), channel_id=1, source_target_pairs={{0,1},{1,2},{2,3},{3,16},{16,17},{17,18},{18,19},{4,5},{5,6},{6,7}... | collective-permute-start | bytes 417800 | tf_op jit(solution)/shard_map/ppermute | solution.py:22
  305.0 10.6 %copy-start.1 = (bf16[2,6]{1,0:T(2,128)(2,1)S(1)}, bf16[2,6]{1,0:T(2,128)(2,1)}, u32[]{:S(2)}) copy-start(bf16[2,6]{1,0:T(2,128)(2,1)} %param.13) | copy-start | bytes 76
Sparse Core Ops, SparseCore 0:
  234.2 18.0 all-gather.6
  280.3 20.0 all-gather.4
